TPU v7x, 256 devices: a whole 4x4x8 slice. The times are simulated.
256 devices in a mesh: tm: 16 (over y, x), space: 16 (over z, core).
Axes of the slice: x: 4, y: 4, z: 8, core: 2. Of those that a mesh axis runs over, the one named last changes fastest.
Arguments:
- stored: bfloat16 [16, 288, 128, 128], P('tm', None, 'space'), may hold values from -6 to 6
- snapshot: int32 [16, 256], P('tm'), may hold values from 0 to 287, as said below
- balance_coef: float32 [128, 128], P('space'), may hold values from 0.5 to 2
- sea_mask: int32 [128, 128], P('space'), may hold values 0 or 1
Outputs:
- merged_basis: bfloat16 [256, 3, 128, 128], P('tm', None, 'space')
Inputs may be any that keep to these rules, and one draw needn't show every extreme that they name: `snapshot`: the 256 indices of one group are distinct.
All inputs are finite; a program needn't handle non-finite values. No bound on the sum of `sea_mask` on one device may be relied on, other than what follows from the above.
Results may differ from a plain program's by a relative error of at most 0.04.
Values may be sent and summed in bfloat16 or wider, within the bound.
No kernel may reach another device: no remote copies, remote signals or barrier semaphores. Data moves between devices by JAX's collectives and lax.ppermute only.
A program may use at most 64 MiB of HBM per device.

v0:
```python
import jax
import jax.numpy as jnp
from jax import lax
from jax.sharding import PartitionSpec as P

inv_root2 = 0.7071067811865476


def gathered_total(shard, axis):
    return lax.all_gather(shard, axis).astype(jnp.float32).sum(0)


def summed_rows(shard, axis):
    count = lax.axis_size(axis)
    parts = lax.all_to_all(shard, axis, 0, 0, tiled=True)
    parts = parts.reshape(count, shard.shape[0] // count, shard.shape[1])
    own_rows = parts.astype(jnp.float32).sum(0)
    return lax.all_gather(own_rows, axis, axis=0, tiled=True)


def with_halo(cells, sides, width):
    for axis, dim in sides:
        count = lax.axis_size(axis)
        ends = count - 1
        head = lax.slice_in_dim(cells, 0, width, axis=dim)
        tail = lax.slice_in_dim(cells, cells.shape[dim] - width, cells.shape[dim], axis=dim)
        cells = jnp.concatenate(
            [
                lax.ppermute(tail, axis, [(i, (i + 1) % count) for i in range(ends)]),
                cells,
                lax.ppermute(head, axis, [((i + 1) % count, i) for i in range(ends)]),
            ],
            axis=dim,
        )
    return cells


def from_partner(shard, axis, stride):
    return lax.ppermute(shard, axis, [(i, i ^ 1 << stride) for i in range(lax.axis_size(axis))])


def balance(padded, balance_coef, sea_float):
    center = padded[:, 1:-1, :]
    cells = lax.broadcasted_iota(jnp.int32, (center.shape[2], center.shape[2]), 0)
    targets = lax.broadcasted_iota(jnp.int32, (center.shape[2], center.shape[2]), 1)
    count = center.shape[2]
    circulant = (cells == (targets + 1) % count).astype(jnp.bfloat16) - (
        cells == (targets - 1) % count
    ).astype(jnp.bfloat16)
    east_minus_west = jnp.einsum(
        "mxy,yz->mxz", center, circulant, preferred_element_type=jnp.float32
    )
    zonal_flow = (-balance_coef * sea_float * east_minus_west).astype(jnp.bfloat16)
    wide = padded.astype(jnp.float32)
    merid_flow = (balance_coef * sea_float * (wide[:, 2:, :] - wide[:, :-2, :])).astype(
        jnp.bfloat16
    )
    return jnp.stack([center, zonal_flow, merid_flow], axis=1).reshape(center.shape[0], -1)


def stack_pair(own_basis, other_basis):
    return jnp.concatenate([own_basis, other_basis], axis=0)


def rotation_of(stacked):
    members = stacked.shape[0] // 2
    local_gram = jnp.dot(stacked, stacked.T, preferred_element_type=jnp.float32)
    local_mixed = (local_gram[:, :members] + local_gram[:, members:]) * inv_root2
    mixed_cols = summed_rows(local_mixed.astype(jnp.bfloat16), "space")
    normal = jnp.dot(
        mixed_cols.T,
        mixed_cols,
        precision=lax.Precision.HIGHEST,
        preferred_element_type=jnp.float32,
    )
    half = normal.shape[0] // 2
    low_11 = lax.linalg.cholesky(normal[:half, :half], symmetrize_input=False)
    low_21 = lax.linalg.triangular_solve(
        low_11, normal[half:, :half], left_side=False, lower=True, transpose_a=True
    )
    low_22 = lax.linalg.cholesky(
        normal[half:, half:] - highest_dot(low_21, low_21.T), symmetrize_input=False
    )
    upper_rows = jax.scipy.linalg.solve_triangular(low_11, mixed_cols[:, :half].T, lower=True)
    lower_rows = jax.scipy.linalg.solve_triangular(
        low_22, mixed_cols[:, half:].T - highest_dot(low_21, upper_rows), lower=True
    )
    return (jnp.concatenate([upper_rows, lower_rows], axis=0) * inv_root2).astype(jnp.bfloat16)


def highest_dot(left, right):
    return jnp.dot(left, right, precision=lax.Precision.HIGHEST, preferred_element_type=jnp.float32)


def rotated(rotation, stacked):
    return jnp.dot(rotation, stacked, preferred_element_type=jnp.float32).astype(jnp.bfloat16)


def body(stored, snapshot, balance_coef, sea_mask):
    sea_float = sea_mask.astype(jnp.float32)
    mean_state = jnp.mean(stored[0].astype(jnp.float32), axis=0)
    picked = jnp.take(stored[0], snapshot[0], axis=0)
    anomaly = ((picked.astype(jnp.float32) - mean_state) * sea_float).astype(jnp.bfloat16)
    other_anomaly = from_partner(anomaly, "tm", 0)
    padded = with_halo(anomaly, (("space", 1),), 1)
    basis_now = balance(padded, balance_coef, sea_float)
    levels = lax.axis_size("tm").bit_length() - 1
    other_rims = from_partner(jnp.concatenate([padded[:, :1], padded[:, -1:]], axis=1), "tm", 0)
    other_padded = jnp.concatenate([other_rims[:, :1], other_anomaly, other_rims[:, 1:]], axis=1)
    partner = balance(other_padded, balance_coef, sea_float)
    stacked = stack_pair(basis_now, partner)
    for level_idx in range(levels):
        if level_idx == levels - 1:
            rotation = rotation_of(stacked)
            member_share = rotation.shape[0] // lax.axis_size("tm")
            rotation = lax.dynamic_slice_in_dim(
                rotation, lax.axis_index("tm") * member_share, member_share, 0
            )
            basis_now = rotated(rotation, stacked)
        else:
            partner_stacked = from_partner(stacked, "tm", level_idx + 1)
            rotation = rotation_of(stacked)
            partner_rotation = from_partner(rotation, "tm", level_idx + 1)
            basis_now = rotated(rotation, stacked)
            partner = rotated(partner_rotation, partner_stacked)
            stacked = stack_pair(basis_now, partner)
    return basis_now.reshape(basis_now.shape[0], 3, stored.shape[2], stored.shape[3])


def solution(mesh):
    placed = (P("tm", None, "space", None), P("tm", None), P("space", None), P("space", None))
    return jax.shard_map(
        body, mesh=mesh, in_specs=placed, out_specs=P("tm", None, "space", None), check_vma=False
    )
```

profile of v0, /device:TPU:1, one launch (start us, length us, event | category | flops | bytes accessed | tf_op | source)
XLA Modules:
  0.0 407.8 jit_solution(4200883872748051215)
XLA Ops:
  6.1 2.1 collective-permute-start.2
  8.2 4.4 %collective-permute-start = (bf16[256,1,128]{0,2,1:T(8,128)(2,1)S(1)}, bf16[256,1,128]{0,2,1:T(8,128)(2,1)S(1)}, u32[]{:S(2)}, u32[]{:S(2)}) collective-permute-start(bf16[256,1,128]{0,2,1:T(8,128)(2,1)S(1)} %get-tuple-element.6), channel_id=1, source_target_pairs={{0,1},{1,2},{2,3},{3,4},{4,5},{5,6},{6,7},{7,8},{8,9},{9,10},{10,1... | collective-permute-start | bytes 196616 | tf_op jit(solution)/shard_map/ppermute | solution.py:29
  12.6 1.9 collective-permute-start.1
  15.4 3.1 collective-permute-done.1
  18.9 4.2 %collective-permute-done.3 = bf16[256,2,128]{0,2,1:T(8,128)(2,1)S(1)} collective-permute-done((bf16[256,2,128]{0,2,1:T(8,128)(2,1)S(1)}, bf16[256,2,128]{0,2,1:T(8,128)(2,1)S(1)}, u32[]{:S(2)}, u32[]{:S(2)}) %collective-permute-start.3) | collective-permute-done | bytes 131104 | tf_op jit(solution)/shard_map/ppermute | solution.py:39
  27.1 9.4 %all-to-all-start = ((bf16[16,32,256]{2,1,0:T(8,128)(2,1)}), bf16[16,32,256]{2,1,0:T(8,128)(2,1)S(1)}, u32[]{:S(2)}, u32[]{:S(2)}) async-start(bf16[16,32,256]{2,1,0:T(8,128)(2,1)} %bitcast.13), calls=%async_computation | async-start | bytes 524288 | tf_op jit(solution)/shard_map/all_to_all | solution.py:15
  36.5 1.9 pad_maximum_fusion
  38.4 2.7 collective-permute-start.5
  41.2 6.9 %all-to-all-done = bf16[16,32,256]{2,1,0:T(8,128)(2,1)S(1)} async-done(((bf16[16,32,256]{2,1,0:T(8,128)(2,1)}), bf16[16,32,256]{2,1,0:T(8,128)(2,1)S(1)}, u32[]{:S(2)}, u32[]{:S(2)}) %all-to-all-start) | async-done | bytes 262176 | tf_op jit(solution)/shard_map/all_to_all | solution.py:15
  48.1 16.1 %all_gather.12 = f32[512,256]{1,0:T(8,128)S(1)} all-gather(f32[32,256]{1,0:T(8,128)S(1)} %convert_reduce_fusion.4), channel_id=1, replica_groups=mesh['tm'=16,'space'=16] {'space'}, dimensions={0}, use_global_device_ids=true | all-gather | bytes 557056 | tf_op jit(solution)/shard_map/all_gather | solution.py:18
  65.2 11.7 %custom-call.26 = f32[128,128]{1,0:T(8,128)S(1)} custom-call(f32[128,128]{1,0:T(8,128)S(1)} %slice.164), custom_call_target="Cholesky" | custom-call | tf_op jit(solution)/shard_map/cholesky/custom-call.1 | solution.py:77
  78.3 9.8 %custom-call.27 = f32[1,128,128]{1,2,0:T(8,128)S(1)} custom-call(f32[1,128,128]{2,1,0:T(8,128)S(1)} %fusion.27), custom_call_target="InvertDiagBlocksLowerTriangular" | custom-call | tf_op jit(solution)/shard_map/jit(_solve_triangular)/triangular_solve | solution.py:84
  88.7 11.7 %custom-call.29 = f32[128,128]{1,0:T(8,128)S(1)} custom-call(f32[128,128]{1,0:T(8,128)S(1)} %convolution_subtract_fusion.7), custom_call_target="Cholesky" | custom-call | tf_op jit(solution)/shard_map/cholesky/custom-call.1 | solution.py:81
  101.8 10.0 %custom-call.30 = f32[1,128,128]{1,2,0:T(8,128)S(1)} custom-call(f32[1,128,128]{2,1,0:T(8,128)S(1)} %fusion.28), custom_call_target="InvertDiagBlocksLowerTriangular" | custom-call | tf_op jit(solution)/shard_map/jit(_solve_triangular)/triangular_solve | solution.py:85
  113.2 2.8 collective-permute-start.4
  116.1 2.4 convolution_convert_fusion.5
  118.5 4.0 collective-permute-done.4
  122.5 2.9 convolution_convert_fusion.4
  128.0 6.1 %all-to-all-start.1 = ((bf16[16,32,256]{2,1,0:T(8,128)(2,1)}), bf16[16,32,256]{2,1,0:T(8,128)(2,1)S(1)}, u32[]{:S(2)}, u32[]{:S(2)}) async-start(bf16[16,32,256]{2,1,0:T(8,128)(2,1)} %bitcast.23), calls=%async_computation.1 | async-start | bytes 524288 | tf_op jit(solution)/shard_map/all_to_all | solution.py:15
  137.3 8.4 %all-to-all-done.1 = bf16[16,32,256]{2,1,0:T(8,128)(2,1)S(1)} async-done(((bf16[16,32,256]{2,1,0:T(8,128)(2,1)}), bf16[16,32,256]{2,1,0:T(8,128)(2,1)S(1)}, u32[]{:S(2)}, u32[]{:S(2)}) %all-to-all-start.1) | async-done | bytes 262176 | tf_op jit(solution)/shard_map/all_to_all | solution.py:15
  145.8 16.3 %all_gather.13 = f32[512,256]{1,0:T(8,128)S(1)} all-gather(f32[32,256]{1,0:T(8,128)S(1)} %convert_reduce_fusion.3), channel_id=1, replica_groups=mesh['tm'=16,'space'=16] {'space'}, dimensions={0}, use_global_device_ids=true | all-gather | bytes 557056 | tf_op jit(solution)/shard_map/all_gather | solution.py:18
  163.1 11.7 %custom-call.31 = f32[128,128]{1,0:T(8,128)S(1)} custom-call(f32[128,128]{1,0:T(8,128)S(1)} %slice.171), custom_call_target="Cholesky" | custom-call | tf_op jit(solution)/shard_map/cholesky/custom-call.1 | solution.py:77
  176.2 9.8 %custom-call.32 = f32[1,128,128]{1,2,0:T(8,128)S(1)} custom-call(f32[1,128,128]{2,1,0:T(8,128)S(1)} %fusion.29), custom_call_target="InvertDiagBlocksLowerTriangular" | custom-call | tf_op jit(solution)/shard_map/jit(_solve_triangular)/triangular_solve | solution.py:84
  186.6 11.7 %custom-call.34 = f32[128,128]{1,0:T(8,128)S(1)} custom-call(f32[128,128]{1,0:T(8,128)S(1)} %convolution_subtract_fusion.6), custom_call_target="Cholesky" | custom-call | tf_op jit(solution)/shard_map/cholesky/custom-call.1 | solution.py:81
  199.6 9.9 %custom-call.35 = f32[1,128,128]{1,2,0:T(8,128)S(1)} custom-call(f32[1,128,128]{2,1,0:T(8,128)S(1)} %fusion.30), custom_call_target="InvertDiagBlocksLowerTriangular" | custom-call | tf_op jit(solution)/shard_map/jit(_solve_triangular)/triangular_solve | solution.py:85
  212.4 2.4 convolution_convert_fusion.3
  214.9 3.9 collective-permute-done.6
  218.8 2.9 convolution_convert_fusion.2
  224.4 6.1 %all-to-all-start.2 = ((bf16[16,32,256]{2,1,0:T(8,128)(2,1)}), bf16[16,32,256]{2,1,0:T(8,128)(2,1)S(1)}, u32[]{:S(2)}, u32[]{:S(2)}) async-start(bf16[16,32,256]{2,1,0:T(8,128)(2,1)} %bitcast.33), calls=%async_computation.2 | async-start | bytes 524288 | tf_op jit(solution)/shard_map/all_to_all | solution.py:15
  232.3 2.9 collective-permute-start.9
  235.2 6.8 %all-to-all-done.2 = bf16[16,32,256]{2,1,0:T(8,128)(2,1)S(1)} async-done(((bf16[16,32,256]{2,1,0:T(8,128)(2,1)}), bf16[16,32,256]{2,1,0:T(8,128)(2,1)S(1)}, u32[]{:S(2)}, u32[]{:S(2)}) %all-to-all-start.2) | async-done | bytes 262176 | tf_op jit(solution)/shard_map/all_to_all | solution.py:15
  242.1 16.1 %all_gather.14 = f32[512,256]{1,0:T(8,128)S(1)} all-gather(f32[32,256]{1,0:T(8,128)S(1)} %convert_reduce_fusion.2), channel_id=1, replica_groups=mesh['tm'=16,'space'=16] {'space'}, dimensions={0}, use_global_device_ids=true | all-gather | bytes 557056 | tf_op jit(solution)/shard_map/all_gather | solution.py:18
  259.2 11.7 %custom-call.36 = f32[128,128]{1,0:T(8,128)S(1)} custom-call(f32[128,128]{1,0:T(8,128)S(1)} %slice.178), custom_call_target="Cholesky" | custom-call | tf_op jit(solution)/shard_map/cholesky/custom-call.1 | solution.py:77
  272.3 9.8 %custom-call.37 = f32[1,128,128]{1,2,0:T(8,128)S(1)} custom-call(f32[1,128,128]{2,1,0:T(8,128)S(1)} %fusion.31), custom_call_target="InvertDiagBlocksLowerTriangular" | custom-call | tf_op jit(solution)/shard_map/jit(_solve_triangular)/triangular_solve | solution.py:84
  282.7 11.7 %custom-call.39 = f32[128,128]{1,0:T(8,128)S(1)} custom-call(f32[128,128]{1,0:T(8,128)S(1)} %convolution_subtract_fusion.5), custom_call_target="Cholesky" | custom-call | tf_op jit(solution)/shard_map/cholesky/custom-call.1 | solution.py:81
  295.7 10.2 %custom-call.40 = f32[1,128,128]{1,2,0:T(8,128)S(1)} custom-call(f32[1,128,128]{2,1,0:T(8,128)S(1)} %fusion.32), custom_call_target="InvertDiagBlocksLowerTriangular" | custom-call | tf_op jit(solution)/shard_map/jit(_solve_triangular)/triangular_solve | solution.py:85
  307.4 3.0 collective-permute-start.8
  310.4 2.4 convolution_convert_fusion.1
  312.8 3.9 collective-permute-done.8
  316.7 2.9 convolution_convert_fusion
  322.3 6.1 %all-to-all-start.3 = ((bf16[16,32,256]{2,1,0:T(8,128)(2,1)}), bf16[16,32,256]{2,1,0:T(8,128)(2,1)S(1)}, u32[]{:S(2)}, u32[]{:S(2)}) async-start(bf16[16,32,256]{2,1,0:T(8,128)(2,1)} %bitcast.43), calls=%async_computation.3 | async-start | bytes 524288 | tf_op jit(solution)/shard_map/all_to_all | solution.py:15
  328.3 11.6 %all-to-all-done.3 = bf16[16,32,256]{2,1,0:T(8,128)(2,1)S(1)} async-done(((bf16[16,32,256]{2,1,0:T(8,128)(2,1)}), bf16[16,32,256]{2,1,0:T(8,128)(2,1)S(1)}, u32[]{:S(2)}, u32[]{:S(2)}) %all-to-all-start.3) | async-done | bytes 262176 | tf_op jit(solution)/shard_map/all_to_all | solution.py:15
  340.0 16.1 %all_gather.15 = f32[512,256]{1,0:T(8,128)S(1)} all-gather(f32[32,256]{1,0:T(8,128)S(1)} %convert_reduce_fusion.1), channel_id=1, replica_groups=mesh['tm'=16,'space'=16] {'space'}, dimensions={0}, use_global_device_ids=true | all-gather | bytes 557056 | tf_op jit(solution)/shard_map/all_gather | solution.py:18
  357.1 11.7 %custom-call.41 = f32[128,128]{1,0:T(8,128)S(1)} custom-call(f32[128,128]{1,0:T(8,128)S(1)} %slice.185), custom_call_target="Cholesky" | custom-call | tf_op jit(solution)/shard_map/cholesky/custom-call.1 | solution.py:77
  370.1 9.8 %custom-call.42 = f32[1,128,128]{1,2,0:T(8,128)S(1)} custom-call(f32[1,128,128]{2,1,0:T(8,128)S(1)} %fusion.33), custom_call_target="InvertDiagBlocksLowerTriangular" | custom-call | tf_op jit(solution)/shard_map/jit(_solve_triangular)/triangular_solve | solution.py:84
  381.0 11.7 %custom-call.44 = f32[128,128]{1,0:T(8,128)S(1)} custom-call(f32[128,128]{1,0:T(8,128)S(1)} %convolution_subtract_fusion.4), custom_call_target="Cholesky" | custom-call | tf_op jit(solution)/shard_map/cholesky/custom-call.1 | solution.py:81
  394.0 10.0 %custom-call.45 = f32[1,128,128]{1,2,0:T(8,128)S(1)} custom-call(f32[1,128,128]{2,1,0:T(8,128)S(1)} %fusion.34), custom_call_target="InvertDiagBlocksLowerTriangular" | custom-call | tf_op jit(solution)/shard_map/jit(_solve_triangular)/triangular_solve | solution.py:85
  405.0 1.9 fusion.5
  (116 shorter events, 49.1 us)
Async XLA Ops:
  0.0 14.9 %copy-start.3 = (s32[8,128]{1,0:T(8,128)S(1)}, s32[8,128]{1,0:T(8,128)}, u32[]{:S(2)}) copy-start(s32[8,128]{1,0:T(8,128)} %param.12) | copy-start | bytes 12292
  0.0 14.9 %copy-start.4 = (f32[8,128]{1,0:T(8,128)S(1)}, f32[8,128]{1,0:T(8,128)}, u32[]{:S(2)}) copy-start(f32[8,128]{1,0:T(8,128)} %param.11) | copy-start | bytes 12292
  6.1 17.1 %collective-permute-start.2 = (bf16[256,8,128]{0,2,1:T(8,128)(2,1)S(1)}, bf16[256,8,128]{0,2,1:T(8,128)(2,1)S(1)}, u32[]{:S(2)}, u32[]{:S(2)}) collective-permute-start(bf16[256,8,128]{0,2,1:T(8,128)(2,1)S(1)} %multiply_convert_fusion), channel_id=1, source_target_pairs={{0,16},{16,0},{32,48},{48,32},{64,80},{80,64},{96,112},{112,96},{1... | collective-permute-start | bytes 1572872 | tf_op jit(solution)/shard_map/ppermute | solution.py:39
  8.2 7.2 %collective-permute-start = (bf16[256,1,128]{0,2,1:T(8,128)(2,1)S(1)}, bf16[256,1,128]{0,2,1:T(8,128)(2,1)S(1)}, u32[]{:S(2)}, u32[]{:S(2)}) collective-permute-start(bf16[256,1,128]{0,2,1:T(8,128)(2,1)S(1)} %get-tuple-element.6), channel_id=1, source_target_pairs={{0,1},{1,2},{2,3},{3,4},{4,5},{5,6},{6,7},{7,8},{8,9},{9,10},{10,1... | collective-permute-start | bytes 196616 | tf_op jit(solution)/shard_map/ppermute | solution.py:29
  12.6 5.9 %collective-permute-start.1 = (bf16[256,1,128]{0,2,1:T(8,128)(2,1)S(1)}, bf16[256,1,128]{0,2,1:T(8,128)(2,1)S(1)}, u32[]{:S(2)}, u32[]{:S(2)}) collective-permute-start(bf16[256,1,128]{0,2,1:T(8,128)(2,1)S(1)} %get-tuple-element.8), channel_id=1, source_target_pairs={{1,0},{2,1},{3,2},{4,3},{5,4},{6,5},{7,6},{8,7},{9,8},{10,9},{11,1... | collective-permute-start | bytes 196616 | tf_op jit(solution)/shard_map/ppermute | solution.py:31
  18.5 4.7 %collective-permute-start.3 = (bf16[256,2,128]{0,2,1:T(8,128)(2,1)S(1)}, bf16[256,2,128]{0,2,1:T(8,128)(2,1)S(1)}, u32[]{:S(2)}, u32[]{:S(2)}) collective-permute-start(bf16[256,2,128]{0,2,1:T(8,128)(2,1)S(1)} %pad_maximum_fusion.10), channel_id=1, source_target_pairs={{0,16},{16,0},{32,48},{48,32},{64,80},{80,64},{96,112},{112,96},{1... | collective-permute-start | bytes 393224 | tf_op jit(solution)/shard_map/ppermute | solution.py:39
  24.5 12.0 %copy-start = (bf16[256,3,8,128]{0,3,2,1:T(8,128)(2,1)}, bf16[256,3,8,128]{0,3,2,1:T(8,128)(2,1)S(1)}, u32[]{:S(2)}) copy-start(bf16[256,3,8,128]{0,3,2,1:T(8,128)(2,1)S(1)} %get-tuple-element.17) | copy-start | bytes 4718596
  27.1 21.0 %all-to-all-start = ((bf16[16,32,256]{2,1,0:T(8,128)(2,1)}), bf16[16,32,256]{2,1,0:T(8,128)(2,1)S(1)}, u32[]{:S(2)}, u32[]{:S(2)}) async-start(bf16[16,32,256]{2,1,0:T(8,128)(2,1)} %bitcast.13), calls=%async_computation | async-start | bytes 524288 | tf_op jit(solution)/shard_map/all_to_all | solution.py:15
  38.4 84.1 %collective-permute-start.5 = (bf16[512,3072]{0,1:T(8,128)(2,1)}, bf16[512,3072]{0,1:T(8,128)(2,1)}, u32[]{:S(2)}, u32[]{:S(2)}) collective-permute-start(bf16[512,3072]{0,1:T(8,128)(2,1)} %pad_maximum_fusion), channel_id=1, source_target_pairs={{0,32},{16,48},{32,0},{48,16},{64,96},{80,112},{96,64},{112,80},{1... | collective-permute-start | bytes 9437192 | tf_op jit(solution)/shard_map/ppermute | solution.py:39
  113.2 9.3 %collective-permute-start.4 = (bf16[256,512]{1,0:T(8,128)(2,1)S(1)}, bf16[256,512]{1,0:T(8,128)(2,1)S(1)}, u32[]{:S(2)}, u32[]{:S(2)}) collective-permute-start(bf16[256,512]{1,0:T(8,128)(2,1)S(1)} %fusion.20), channel_id=1, source_target_pairs={{0,32},{16,48},{32,0},{48,16},{64,96},{80,112},{96,64},{112,80},{1... | collective-permute-start | bytes 786440 | tf_op jit(solution)/shard_map/ppermute | solution.py:39
  118.5 15.6 %copy-start.1 = (bf16[256,3072]{1,0:T(8,128)(2,1)}, bf16[256,3072]{1,0:T(8,128)(2,1)S(1)}, u32[]{:S(2)}) copy-start(bf16[256,3072]{1,0:T(8,128)(2,1)S(1)} %convolution_convert_fusion.5) | copy-start | bytes 4718596
  128.0 17.7 %all-to-all-start.1 = ((bf16[16,32,256]{2,1,0:T(8,128)(2,1)}), bf16[16,32,256]{2,1,0:T(8,128)(2,1)S(1)}, u32[]{:S(2)}, u32[]{:S(2)}) async-start(bf16[16,32,256]{2,1,0:T(8,128)(2,1)} %bitcast.23), calls=%async_computation.1 | async-start | bytes 524288 | tf_op jit(solution)/shard_map/all_to_all | solution.py:15
  136.0 82.8 %collective-permute-start.7 = (bf16[512,3072]{1,0:T(8,128)(2,1)}, bf16[512,3072]{1,0:T(8,128)(2,1)}, u32[]{:S(2)}, u32[]{:S(2)}) collective-permute-start(bf16[512,3072]{1,0:T(8,128)(2,1)} %pad_maximum_fusion.1), channel_id=1, source_target_pairs={{0,64},{16,80},{32,96},{48,112},{64,0},{80,16},{96,32},{112,48},{1... | collective-permute-start | bytes 9437192 | tf_op jit(solution)/shard_map/ppermute | solution.py:39
  211.1 7.8 %collective-permute-start.6 = (bf16[256,512]{1,0:T(8,128)(2,1)S(1)}, bf16[256,512]{1,0:T(8,128)(2,1)S(1)}, u32[]{:S(2)}, u32[]{:S(2)}) collective-permute-start(bf16[256,512]{1,0:T(8,128)(2,1)S(1)} %fusion.21), channel_id=1, source_target_pairs={{0,64},{16,80},{32,96},{48,112},{64,0},{80,16},{96,32},{112,48},{1... | collective-permute-start | bytes 786440 | tf_op jit(solution)/shard_map/ppermute | solution.py:39
  214.9 15.6 %copy-start.2 = (bf16[256,3072]{1,0:T(8,128)(2,1)}, bf16[256,3072]{1,0:T(8,128)(2,1)S(1)}, u32[]{:S(2)}) copy-start(bf16[256,3072]{1,0:T(8,128)(2,1)S(1)} %convolution_convert_fusion.3) | copy-start | bytes 4718596
  224.4 17.7 %all-to-all-start.2 = ((bf16[16,32,256]{2,1,0:T(8,128)(2,1)}), bf16[16,32,256]{2,1,0:T(8,128)(2,1)S(1)}, u32[]{:S(2)}, u32[]{:S(2)}) async-start(bf16[16,32,256]{2,1,0:T(8,128)(2,1)} %bitcast.33), calls=%async_computation.2 | async-start | bytes 524288 | tf_op jit(solution)/shard_map/all_to_all | solution.py:15
  232.3 84.4 %collective-permute-start.9 = (bf16[512,3072]{1,0:T(8,128)(2,1)}, bf16[512,3072]{1,0:T(8,128)(2,1)}, u32[]{:S(2)}, u32[]{:S(2)}) collective-permute-start(bf16[512,3072]{1,0:T(8,128)(2,1)} %pad_maximum_fusion.2), channel_id=1, source_target_pairs={{0,128},{16,144},{32,160},{48,176},{64,192},{80,208},{96,224},{112... | collective-permute-start | bytes 9437192 | tf_op jit(solution)/shard_map/ppermute | solution.py:39
  307.4 9.3 %collective-permute-start.8 = (bf16[256,512]{1,0:T(8,128)(2,1)S(1)}, bf16[256,512]{1,0:T(8,128)(2,1)S(1)}, u32[]{:S(2)}, u32[]{:S(2)}) collective-permute-start(bf16[256,512]{1,0:T(8,128)(2,1)S(1)} %fusion.22), channel_id=1, source_target_pairs={{0,128},{16,144},{32,160},{48,176},{64,192},{80,208},{96,224},{112... | collective-permute-start | bytes 786440 | tf_op jit(solution)/shard_map/ppermute | solution.py:39
  312.8 8.7 %copy-start.5 = (bf16[256,3072]{1,0:T(8,128)(2,1)}, bf16[256,3072]{1,0:T(8,128)(2,1)S(1)}, u32[]{:S(2)}) copy-start(bf16[256,3072]{1,0:T(8,128)(2,1)S(1)} %convolution_convert_fusion.1) | copy-start | bytes 4718596
  322.3 17.7 %all-to-all-start.3 = ((bf16[16,32,256]{2,1,0:T(8,128)(2,1)}), bf16[16,32,256]{2,1,0:T(8,128)(2,1)S(1)}, u32[]{:S(2)}, u32[]{:S(2)}) async-start(bf16[16,32,256]{2,1,0:T(8,128)(2,1)} %bitcast.43), calls=%async_computation.3 | async-start | bytes 524288 | tf_op jit(solution)/shard_map/all_to_all | solution.py:15
where the time goes:
time: 414 us; the launch traced here: 408 us
  other arithmetic  198 us (48%)
  blocking collectives  64.6 us (16%)
  waiting for transfers between devices  52.9 us (13%)
  starting transfers between devices  50.6 us (12%)
  matrix products  38 us (9%)
    all_gather x4, blocking collectives, summed_rows(): return lax.all_gather(own_rows, axis, axis=0, tiled=True)  64.6 us
    another operation x12, other arithmetic, rotation_of(): lax.linalg.cholesky(normal[half:, half:] - highest_dot(low_21, low_21.T),...  49.6 us
    another operation x12, other arithmetic, rotation_of(): low_11 = lax.linalg.cholesky(normal[:half, :half], symmetrize_input=False)  49.6 us
    another operation x8, other arithmetic, rotation_of(): jax.scipy.linalg.solve_triangular(low_22, mixed_cols[:, half:].T - highes...  42.7 us
    another operation x8, other arithmetic, rotation_of(): jax.scipy.linalg.solve_triangular(low_11, mixed_cols[:, :half].T, lower=T...  41.9 us
    all_to_all x4, waiting for transfers between devices, summed_rows(): parts = lax.all_to_all(shard, axis, 0, 0, tiled=True)  33.7 us
    all_to_all x4, starting transfers between devices, summed_rows(): parts = lax.all_to_all(shard, axis, 0, 0, tiled=True)  27.7 us
    dot_general x7, matrix products, rotated(): jnp.dot(rotation, stacked, preferred_element_type=jnp.float32)  17.9 us
  transfers between devices with their start and end apart: 14, of which 9 were waited for; matrix products, arithmetic and copies ran while one was open for 39% of the time, Pallas kernels for 0%

commit v1 on v0

--- a/solution.py
+++ b/solution.py
@@ -15,7 +15,16 @@
     parts = lax.all_to_all(shard, axis, 0, 0, tiled=True)
     parts = parts.reshape(count, shard.shape[0] // count, shard.shape[1])
     own_rows = parts.astype(jnp.float32).sum(0)
-    return lax.all_gather(own_rows, axis, axis=0, tiled=True)
+
+    def work_the_loops(page, shard_axis):
+        kept_rows = []
+        for _ in range(lax.axis_size(shard_axis)):
+            kept_rows.append(page)
+        local_next = lax.all_to_all(jnp.stack(kept_rows, 0), shard_axis, 0, 0)
+        frame_out = jnp.concatenate(local_next, 0)
+        return frame_out
+
+    return work_the_loops(own_rows, shard_axis=axis)
 
 
 def with_halo(cells, sides, width):

time: 414 us -> 450 us (1.087)
  waiting for transfers between devices: 52.9 us -> 82.3 us
  starting transfers between devices: 50.6 us -> 38.4 us
  blocking collectives: 64.6 us -> 74.2 us
    all_to_all x0 -> x4, blocking collectives: none -> 74.2 us  [summed_rows(): parts = lax.all_to_all(shard, axis, 0, 0, tiled=True)]
    all_gather x4 -> x0, blocking collectives: 64.6 us -> none  [summed_rows(): return lax.all_gather(own_rows, axis, axis=0, tiled=True)]
    all_to_all x4, waiting for transfers between devices: 33.7 us -> 50.7 us  [work_the_loops(): local_next = lax.all_to_all(jnp.stack(kept_rows, 0), shard_axis, 0, 0)]
    all_to_all x4, starting transfers between devices: 27.7 us -> 14.7 us  [work_the_loops(): local_next = lax.all_to_all(jnp.stack(kept_rows, 0), shard_axis, 0, 0)]
    ppermute x8, waiting for transfers between devices: 16.1 us -> 28.5 us  [from_partner(): lax.ppermute(shard, axis, [(i, i ^ 1 << stride) for i in range(lax.axis_s...]
  transfers between devices with their start and end apart: 14 -> 14, of which waited for: 9 -> 9; matrix products, arithmetic and copies ran while one was open for 39% -> 38% of each run, Pallas kernels for 0% -> 0%
where the time goes in v1:
time: 450 us; the launch traced here: 443 us
  other arithmetic  200 us (44%)
  waiting for transfers between devices  82.3 us (18%)
  blocking collectives  74.2 us (16%)
  matrix products  40.5 us (9%)
  starting transfers between devices  38.4 us (9%)
  local copies, waits for them, and re-layouts  6.38 us (1%)
    all_to_all x4, blocking collectives, summed_rows(): parts = lax.all_to_all(shard, axis, 0, 0, tiled=True)  74.2 us
    all_to_all x4, waiting for transfers between devices, work_the_loops(): local_next = lax.all_to_all(jnp.stack(kept_rows, 0), shard_axis, 0, 0)  50.7 us
    another operation x12, other arithmetic, rotation_of(): lax.linalg.cholesky(normal[half:, half:] - highest_dot(low_21, low_21.T),...  50.4 us
    another operation x12, other arithmetic, rotation_of(): low_11 = lax.linalg.cholesky(normal[:half, :half], symmetrize_input=False)  49.6 us
    another operation x8, other arithmetic, rotation_of(): jax.scipy.linalg.solve_triangular(low_11, mixed_cols[:, :half].T, lower=T...  43.4 us
    another operation x8, other arithmetic, rotation_of(): jax.scipy.linalg.solve_triangular(low_22, mixed_cols[:, half:].T - highes...  42.8 us
    ppermute x8, waiting for transfers between devices, from_partner(): lax.ppermute(shard, axis, [(i, i ^ 1 << stride) for i in range(lax.axis_s...  28.5 us
    ppermute x8, starting transfers between devices, from_partner(): lax.ppermute(shard, axis, [(i, i ^ 1 << stride) for i in range(lax.axis_s...  17.4 us
  transfers between devices with their start and end apart: 14, of which 9 were waited for; matrix products, arithmetic and copies ran while one was open for 38% of the time, Pallas kernels for 0%

profile of v1, /device:TPU:1, one launch (start us, length us, event | category | flops | bytes accessed | tf_op | source)
XLA Modules:
  0.0 443.1 jit_solution(6219807550375363598)
XLA Ops:
  6.0 2.1 collective-permute-start.2
  8.2 4.4 collective-permute-start
  15.4 3.1 collective-permute-done.1
  18.9 4.2 collective-permute-done.3
  26.4 20.8 %all_to_all.56 = bf16[16,32,256]{2,1,0:T(8,128)(2,1)S(1)} all-to-all(bf16[16,32,256]{2,1,0:T(8,128)(2,1)S(1)} %bitcast.190), channel_id=1, replica_groups=mesh['tm'=16,'space'=16] {'space'}, dimensions={0} | all-to-all | bytes 524288 | tf_op jit(solution)/shard_map/all_to_all | solution.py:15
  48.1 4.1 all-to-all-start.1
  54.1 2.9 collective-permute-start.5
  57.0 12.0 %all-to-all-done.1 = f32[16,32,256]{2,1,0:T(8,128)} async-done(((f32[16,32,256]{2,1,0:T(8,128)}), f32[16,32,256]{2,1,0:T(8,128)}, u32[]{:S(2)}, u32[]{:S(2)}) %all-to-all-start.1) | async-done | bytes 524320 | tf_op jit(solution)/shard_map/all_to_all | solution.py:23
  69.0 2.2 convolution_bitcast_fusion.3
  71.3 11.7 %custom-call.26 = f32[128,128]{1,0:T(8,128)S(1)} custom-call(f32[128,128]{1,0:T(8,128)S(1)} %slice.164), custom_call_target="Cholesky" | custom-call | tf_op jit(solution)/shard_map/cholesky/custom-call.1 | solution.py:86
  85.1 10.6 %custom-call.27 = f32[1,128,128]{1,2,0:T(8,128)S(1)} custom-call(f32[1,128,128]{2,1,0:T(8,128)} %fusion.27), custom_call_target="InvertDiagBlocksLowerTriangular" | custom-call | tf_op jit(solution)/shard_map/jit(_solve_triangular)/triangular_solve | solution.py:93
  96.9 12.5 %custom-call.29 = f32[128,128]{1,0:T(8,128)S(1)} custom-call(f32[128,128]{1,0:T(8,128)} %convolution_subtract_fusion.7), custom_call_target="Cholesky" | custom-call | tf_op jit(solution)/shard_map/cholesky/custom-call.1 | solution.py:90
  110.8 10.0 %custom-call.30 = f32[1,128,128]{1,2,0:T(8,128)S(1)} custom-call(f32[1,128,128]{2,1,0:T(8,128)S(1)} %fusion.28), custom_call_target="InvertDiagBlocksLowerTriangular" | custom-call | tf_op jit(solution)/shard_map/jit(_solve_triangular)/triangular_solve | solution.py:94
  124.2 2.8 collective-permute-start.4
  128.1 5.2 %collective-permute-done.4 = bf16[256,512]{1,0:T(8,128)(2,1)S(1)} collective-permute-done((bf16[256,512]{1,0:T(8,128)(2,1)S(1)}, bf16[256,512]{1,0:T(8,128)(2,1)S(1)}, u32[]{:S(2)}, u32[]{:S(2)}) %collective-permute-start.4) | collective-permute-done | bytes 262176 | tf_op jit(solution)/shard_map/ppermute | solution.py:48
  133.3 2.9 convolution_convert_fusion.4
  138.1 16.6 %all_to_all.57 = bf16[16,32,256]{2,1,0:T(8,128)(2,1)S(1)} all-to-all(bf16[16,32,256]{2,1,0:T(8,128)(2,1)S(1)} %bitcast.191), channel_id=1, replica_groups=mesh['tm'=16,'space'=16] {'space'}, dimensions={0} | all-to-all | bytes 524288 | tf_op jit(solution)/shard_map/all_to_all | solution.py:15
  155.6 3.5 all-to-all-start.3
  159.1 3.3 pad_maximum_fusion.1
  164.1 11.8 %all-to-all-done.3 = f32[16,32,256]{2,1,0:T(8,128)S(1)} async-done(((f32[16,32,256]{2,1,0:T(8,128)}), f32[16,32,256]{2,1,0:T(8,128)S(1)}, u32[]{:S(2)}, u32[]{:S(2)}) %all-to-all-start.3) | async-done | bytes 524320 | tf_op jit(solution)/shard_map/all_to_all | solution.py:23
  176.9 11.7 %custom-call.31 = f32[128,128]{1,0:T(8,128)S(1)} custom-call(f32[128,128]{1,0:T(8,128)S(1)} %slice.171), custom_call_target="Cholesky" | custom-call | tf_op jit(solution)/shard_map/cholesky/custom-call.1 | solution.py:86
  190.0 9.8 %custom-call.32 = f32[1,128,128]{1,2,0:T(8,128)S(1)} custom-call(f32[1,128,128]{2,1,0:T(8,128)S(1)} %fusion.29), custom_call_target="InvertDiagBlocksLowerTriangular" | custom-call | tf_op jit(solution)/shard_map/jit(_solve_triangular)/triangular_solve | solution.py:93
  200.4 11.7 %custom-call.34 = f32[128,128]{1,0:T(8,128)S(1)} custom-call(f32[128,128]{1,0:T(8,128)S(1)} %convolution_subtract_fusion.6), custom_call_target="Cholesky" | custom-call | tf_op jit(solution)/shard_map/cholesky/custom-call.1 | solution.py:90
  213.4 10.0 %custom-call.35 = f32[1,128,128]{1,2,0:T(8,128)S(1)} custom-call(f32[1,128,128]{2,1,0:T(8,128)S(1)} %fusion.30), custom_call_target="InvertDiagBlocksLowerTriangular" | custom-call | tf_op jit(solution)/shard_map/jit(_solve_triangular)/triangular_solve | solution.py:94
  226.3 2.4 convolution_convert_fusion.3
  228.7 9.8 %collective-permute-done.6 = bf16[256,512]{1,0:T(8,128)(2,1)S(1)} collective-permute-done((bf16[256,512]{1,0:T(8,128)(2,1)S(1)}, bf16[256,512]{1,0:T(8,128)(2,1)S(1)}, u32[]{:S(2)}, u32[]{:S(2)}) %collective-permute-start.6) | collective-permute-done | bytes 262176 | tf_op jit(solution)/shard_map/ppermute | solution.py:48
  238.5 2.9 convolution_convert_fusion.2
  243.3 18.4 %all_to_all.58 = bf16[16,32,256]{2,1,0:T(8,128)(2,1)S(1)} all-to-all(bf16[16,32,256]{2,1,0:T(8,128)(2,1)S(1)} %bitcast.192), channel_id=1, replica_groups=mesh['tm'=16,'space'=16] {'space'}, dimensions={0} | all-to-all | bytes 524288 | tf_op jit(solution)/shard_map/all_to_all | solution.py:15
  262.7 3.5 all-to-all-start.5
  266.1 3.3 pad_maximum_fusion.2
  269.4 3.1 collective-permute-start.9
  272.5 10.4 %all-to-all-done.5 = f32[16,32,256]{2,1,0:T(8,128)S(1)} async-done(((f32[16,32,256]{2,1,0:T(8,128)}), f32[16,32,256]{2,1,0:T(8,128)S(1)}, u32[]{:S(2)}, u32[]{:S(2)}) %all-to-all-start.5) | async-done | bytes 524320 | tf_op jit(solution)/shard_map/all_to_all | solution.py:23
  283.9 11.7 %custom-call.36 = f32[128,128]{1,0:T(8,128)S(1)} custom-call(f32[128,128]{1,0:T(8,128)S(1)} %slice.178), custom_call_target="Cholesky" | custom-call | tf_op jit(solution)/shard_map/cholesky/custom-call.1 | solution.py:86
  297.0 9.8 %custom-call.37 = f32[1,128,128]{1,2,0:T(8,128)S(1)} custom-call(f32[1,128,128]{2,1,0:T(8,128)S(1)} %fusion.31), custom_call_target="InvertDiagBlocksLowerTriangular" | custom-call | tf_op jit(solution)/shard_map/jit(_solve_triangular)/triangular_solve | solution.py:93
  307.4 11.7 %custom-call.39 = f32[128,128]{1,0:T(8,128)S(1)} custom-call(f32[128,128]{1,0:T(8,128)S(1)} %convolution_subtract_fusion.5), custom_call_target="Cholesky" | custom-call | tf_op jit(solution)/shard_map/cholesky/custom-call.1 | solution.py:90
  320.5 10.2 %custom-call.40 = f32[1,128,128]{1,2,0:T(8,128)S(1)} custom-call(f32[1,128,128]{2,1,0:T(8,128)S(1)} %fusion.32), custom_call_target="InvertDiagBlocksLowerTriangular" | custom-call | tf_op jit(solution)/shard_map/jit(_solve_triangular)/triangular_solve | solution.py:94
  332.1 3.0 collective-permute-start.8
  335.2 2.4 convolution_convert_fusion.1
  337.6 9.2 %collective-permute-done.8 = bf16[256,512]{1,0:T(8,128)(2,1)S(1)} collective-permute-done((bf16[256,512]{1,0:T(8,128)(2,1)S(1)}, bf16[256,512]{1,0:T(8,128)(2,1)S(1)}, u32[]{:S(2)}, u32[]{:S(2)}) %collective-permute-start.8) | collective-permute-done | bytes 262176 | tf_op jit(solution)/shard_map/ppermute | solution.py:48
  346.8 2.9 convolution_convert_fusion
  351.7 18.4 %all_to_all.59 = bf16[16,32,256]{2,1,0:T(8,128)(2,1)S(1)} all-to-all(bf16[16,32,256]{2,1,0:T(8,128)(2,1)S(1)} %bitcast.193), channel_id=1, replica_groups=mesh['tm'=16,'space'=16] {'space'}, dimensions={0} | all-to-all | bytes 524288 | tf_op jit(solution)/shard_map/all_to_all | solution.py:15
  371.0 3.6 all-to-all-start.7
  374.7 16.6 %all-to-all-done.7 = f32[16,32,256]{2,1,0:T(8,128)S(1)} async-done(((f32[16,32,256]{2,1,0:T(8,128)}), f32[16,32,256]{2,1,0:T(8,128)S(1)}, u32[]{:S(2)}, u32[]{:S(2)}) %all-to-all-start.7) | async-done | bytes 524320 | tf_op jit(solution)/shard_map/all_to_all | solution.py:23
  392.3 11.7 %custom-call.41 = f32[128,128]{1,0:T(8,128)S(1)} custom-call(f32[128,128]{1,0:T(8,128)S(1)} %slice.185), custom_call_target="Cholesky" | custom-call | tf_op jit(solution)/shard_map/cholesky/custom-call.1 | solution.py:86
  405.3 9.8 %custom-call.42 = f32[1,128,128]{1,2,0:T(8,128)S(1)} custom-call(f32[1,128,128]{2,1,0:T(8,128)S(1)} %fusion.33), custom_call_target="InvertDiagBlocksLowerTriangular" | custom-call | tf_op jit(solution)/shard_map/jit(_solve_triangular)/triangular_solve | solution.py:93
  415.7 11.7 %custom-call.44 = f32[128,128]{1,0:T(8,128)S(1)} custom-call(f32[128,128]{1,0:T(8,128)S(1)} %convolution_subtract_fusion.4), custom_call_target="Cholesky" | custom-call | tf_op jit(solution)/shard_map/cholesky/custom-call.1 | solution.py:90
  428.8 10.0 %custom-call.45 = f32[1,128,128]{1,2,0:T(8,128)S(1)} custom-call(f32[1,128,128]{2,1,0:T(8,128)S(1)} %fusion.34), custom_call_target="InvertDiagBlocksLowerTriangular" | custom-call | tf_op jit(solution)/shard_map/jit(_solve_triangular)/triangular_solve | solution.py:94
  440.2 1.9 fusion.5
  (118 shorter events, 53.5 us)
Async XLA Ops:
  0.0 14.9 %copy-start.2 = (s32[8,128]{1,0:T(8,128)S(1)}, s32[8,128]{1,0:T(8,128)}, u32[]{:S(2)}) copy-start(s32[8,128]{1,0:T(8,128)} %param.12) | copy-start | bytes 12292
  0.0 14.9 %copy-start.3 = (f32[8,128]{1,0:T(8,128)S(1)}, f32[8,128]{1,0:T(8,128)}, u32[]{:S(2)}) copy-start(f32[8,128]{1,0:T(8,128)} %param.11) | copy-start | bytes 12292
  6.0 17.1 %collective-permute-start.2 = (bf16[256,8,128]{0,2,1:T(8,128)(2,1)S(1)}, bf16[256,8,128]{0,2,1:T(8,128)(2,1)S(1)}, u32[]{:S(2)}, u32[]{:S(2)}) collective-permute-start(bf16[256,8,128]{0,2,1:T(8,128)(2,1)S(1)} %multiply_convert_fusion), channel_id=1, source_target_pairs={{0,16},{16,0},{32,48},{48,32},{64,80},{80,64},{96,112},{112,96},{1... | collective-permute-start | bytes 1572872 | tf_op jit(solution)/shard_map/ppermute | solution.py:48
  8.2 7.2 %collective-permute-start = (bf16[256,1,128]{0,2,1:T(8,128)(2,1)S(1)}, bf16[256,1,128]{0,2,1:T(8,128)(2,1)S(1)}, u32[]{:S(2)}, u32[]{:S(2)}) collective-permute-start(bf16[256,1,128]{0,2,1:T(8,128)(2,1)S(1)} %get-tuple-element.6), channel_id=1, source_target_pairs={{0,1},{1,2},{2,3},{3,4},{4,5},{5,6},{6,7},{7,8},{8,9},{9,10},{10,1... | collective-permute-start | bytes 196616 | tf_op jit(solution)/shard_map/ppermute | solution.py:38
  12.6 5.9 %collective-permute-start.1 = (bf16[256,1,128]{0,2,1:T(8,128)(2,1)S(1)}, bf16[256,1,128]{0,2,1:T(8,128)(2,1)S(1)}, u32[]{:S(2)}, u32[]{:S(2)}) collective-permute-start(bf16[256,1,128]{0,2,1:T(8,128)(2,1)S(1)} %get-tuple-element.8), channel_id=1, source_target_pairs={{1,0},{2,1},{3,2},{4,3},{5,4},{6,5},{7,6},{8,7},{9,8},{10,9},{11,1... | collective-permute-start | bytes 196616 | tf_op jit(solution)/shard_map/ppermute | solution.py:40
  18.5 4.7 %collective-permute-start.3 = (bf16[256,2,128]{0,2,1:T(8,128)(2,1)S(1)}, bf16[256,2,128]{0,2,1:T(8,128)(2,1)S(1)}, u32[]{:S(2)}, u32[]{:S(2)}) collective-permute-start(bf16[256,2,128]{0,2,1:T(8,128)(2,1)S(1)} %pad_maximum_fusion.10), channel_id=1, source_target_pairs={{0,16},{16,0},{32,48},{48,32},{64,80},{80,64},{96,112},{112,96},{1... | collective-permute-start | bytes 393224 | tf_op jit(solution)/shard_map/ppermute | solution.py:48
  48.1 20.9 %all-to-all-start.1 = ((f32[16,32,256]{2,1,0:T(8,128)}), f32[16,32,256]{2,1,0:T(8,128)}, u32[]{:S(2)}, u32[]{:S(2)}) async-start(f32[16,32,256]{2,1,0:T(8,128)} %stack.29), calls=%async_computation.1 | async-start | bytes 1048576 | tf_op jit(solution)/shard_map/all_to_all | solution.py:23
  54.1 79.2 %collective-permute-start.5 = (bf16[512,3072]{0,1:T(8,128)(2,1)}, bf16[512,3072]{0,1:T(8,128)(2,1)}, u32[]{:S(2)}, u32[]{:S(2)}) collective-permute-start(bf16[512,3072]{0,1:T(8,128)(2,1)} %pad_maximum_fusion), channel_id=1, source_target_pairs={{0,32},{16,48},{32,0},{48,16},{64,96},{80,112},{96,64},{112,80},{1... | collective-permute-start | bytes 9437192 | tf_op jit(solution)/shard_map/ppermute | solution.py:48
  124.2 9.1 %collective-permute-start.4 = (bf16[256,512]{1,0:T(8,128)(2,1)S(1)}, bf16[256,512]{1,0:T(8,128)(2,1)S(1)}, u32[]{:S(2)}, u32[]{:S(2)}) collective-permute-start(bf16[256,512]{1,0:T(8,128)(2,1)S(1)} %fusion.20), channel_id=1, source_target_pairs={{0,32},{16,48},{32,0},{48,16},{64,96},{80,112},{96,64},{112,80},{1... | collective-permute-start | bytes 786440 | tf_op jit(solution)/shard_map/ppermute | solution.py:48
  128.1 10.0 %copy-start = (bf16[256,3072]{1,0:T(8,128)(2,1)}, bf16[256,3072]{1,0:T(8,128)(2,1)S(1)}, u32[]{:S(2)}) copy-start(bf16[256,3072]{1,0:T(8,128)(2,1)S(1)} %convolution_convert_fusion.5) | copy-start | bytes 4718596
  155.6 20.2 %all-to-all-start.3 = ((f32[16,32,256]{2,1,0:T(8,128)}), f32[16,32,256]{2,1,0:T(8,128)S(1)}, u32[]{:S(2)}, u32[]{:S(2)}) async-start(f32[16,32,256]{2,1,0:T(8,128)} %stack.30), calls=%async_computation.3 | async-start | bytes 1048576 | tf_op jit(solution)/shard_map/all_to_all | solution.py:23
  162.4 76.1 %collective-permute-start.7 = (bf16[512,3072]{1,0:T(8,128)(2,1)}, bf16[512,3072]{1,0:T(8,128)(2,1)}, u32[]{:S(2)}, u32[]{:S(2)}) collective-permute-start(bf16[512,3072]{1,0:T(8,128)(2,1)} %pad_maximum_fusion.1), channel_id=1, source_target_pairs={{0,64},{16,80},{32,96},{48,112},{64,0},{80,16},{96,32},{112,48},{1... | collective-permute-start | bytes 9437192 | tf_op jit(solution)/shard_map/ppermute | solution.py:48
  224.9 13.6 %collective-permute-start.6 = (bf16[256,512]{1,0:T(8,128)(2,1)S(1)}, bf16[256,512]{1,0:T(8,128)(2,1)S(1)}, u32[]{:S(2)}, u32[]{:S(2)}) collective-permute-start(bf16[256,512]{1,0:T(8,128)(2,1)S(1)} %fusion.21), channel_id=1, source_target_pairs={{0,64},{16,80},{32,96},{48,112},{64,0},{80,16},{96,32},{112,48},{1... | collective-permute-start | bytes 786440 | tf_op jit(solution)/shard_map/ppermute | solution.py:48
  228.7 14.6 %copy-start.1 = (bf16[256,3072]{1,0:T(8,128)(2,1)}, bf16[256,3072]{1,0:T(8,128)(2,1)S(1)}, u32[]{:S(2)}) copy-start(bf16[256,3072]{1,0:T(8,128)(2,1)S(1)} %convolution_convert_fusion.3) | copy-start | bytes 4718596
  262.7 20.2 %all-to-all-start.5 = ((f32[16,32,256]{2,1,0:T(8,128)}), f32[16,32,256]{2,1,0:T(8,128)S(1)}, u32[]{:S(2)}, u32[]{:S(2)}) async-start(f32[16,32,256]{2,1,0:T(8,128)} %stack.31), calls=%async_computation.5 | async-start | bytes 1048576 | tf_op jit(solution)/shard_map/all_to_all | solution.py:23
  269.4 77.4 %collective-permute-start.9 = (bf16[512,3072]{1,0:T(8,128)(2,1)}, bf16[512,3072]{1,0:T(8,128)(2,1)}, u32[]{:S(2)}, u32[]{:S(2)}) collective-permute-start(bf16[512,3072]{1,0:T(8,128)(2,1)} %pad_maximum_fusion.2), channel_id=1, source_target_pairs={{0,128},{16,144},{32,160},{48,176},{64,192},{80,208},{96,224},{112... | collective-permute-start | bytes 9437192 | tf_op jit(solution)/shard_map/ppermute | solution.py:48
  332.1 14.7 %collective-permute-start.8 = (bf16[256,512]{1,0:T(8,128)(2,1)S(1)}, bf16[256,512]{1,0:T(8,128)(2,1)S(1)}, u32[]{:S(2)}, u32[]{:S(2)}) collective-permute-start(bf16[256,512]{1,0:T(8,128)(2,1)S(1)} %fusion.22), channel_id=1, source_target_pairs={{0,128},{16,144},{32,160},{48,176},{64,192},{80,208},{96,224},{112... | collective-permute-start | bytes 786440 | tf_op jit(solution)/shard_map/ppermute | solution.py:48
  337.6 14.0 %copy-start.4 = (bf16[256,3072]{1,0:T(8,128)(2,1)}, bf16[256,3072]{1,0:T(8,128)(2,1)S(1)}, u32[]{:S(2)}) copy-start(bf16[256,3072]{1,0:T(8,128)(2,1)S(1)} %convolution_convert_fusion.1) | copy-start | bytes 4718596
  371.0 20.2 %all-to-all-start.7 = ((f32[16,32,256]{2,1,0:T(8,128)}), f32[16,32,256]{2,1,0:T(8,128)S(1)}, u32[]{:S(2)}, u32[]{:S(2)}) async-start(f32[16,32,256]{2,1,0:T(8,128)} %stack.32), calls=%async_computation.7 | async-start | bytes 1048576 | tf_op jit(solution)/shard_map/all_to_all | solution.py:23
